TPU v7x, 512 devices: a whole 4x4x16 slice. The times are simulated.
512 devices in a mesh: seq: 64 (over z, y), tensor: 8 (over x, core).
Axes of the slice: x: 4, y: 4, z: 16, core: 2. Of those that a mesh axis runs over, the one named last changes fastest.
Arguments:
- hidden: bfloat16 [8192, 4096], P('seq', 'tensor')
- norm_gain: bfloat16 [4096], replicated, may hold values from 0.5 to 1.5
- w_query: bfloat16 [4096, 4096], P('seq', 'tensor')
- key_value_weight: bfloat16 [4096, 1024], P('seq')
- w_out: bfloat16 [4096, 4096], P('tensor', 'seq'), may hold values from -0.09375 to 0.09375
- prefix_key_cache: bfloat16 [64, 1024, 1024], P('seq')
- prefix_owner: int32 [64], replicated, may hold values from 0 to 63, each once
- token_counts: int32 [64, 64], P('seq'), may hold values from 0 to 4, as said below
Outputs:
- attn_out: bfloat16 [8192, 4096], P('seq', 'tensor')
- suffix_key_cache: bfloat16 [8192, 1024], P('seq', 'tensor')
Inputs may be any that keep to these rules, and one draw needn't show every extreme that they name: `token_counts`: each row sums to 128; one prefix receives exactly 4 tokens from every sequence index.
All inputs are finite; a program needn't handle non-finite values.
Results may differ from a plain program's by a relative error of at most 0.035.
Values may be sent and summed in bfloat16 or wider, within the bound.
No kernel may reach another device: no remote copies, remote signals or barrier semaphores. Data moves between devices by JAX's collectives and lax.ppermute only.
A program may use at most 64 MiB of HBM per device.

v0:
```python
import jax
import jax.numpy as jnp
from jax import lax
from jax.sharding import PartitionSpec as P

HEAD_DIM = 128
PREFIX_LENGTH = 1024
eps = 1e-06
theta = 5000000.0


def rotate(values, positions):
    half = values.shape[-1] // 2
    frequency = theta ** (-jnp.arange(half, dtype=jnp.float32) * 2.0 / values.shape[-1])
    angle = positions.astype(jnp.float32)[:, None] * frequency[None, :]
    cosine = jnp.cos(angle)[:, None, :]
    sine = jnp.sin(angle)[:, None, :]
    first = values[..., :half]
    second = values[..., half:]
    return jnp.concatenate(
        [first * cosine - second * sine, second * cosine + first * sine], axis=-1
    )


def layout(counts_row, length):
    ends = jnp.cumsum(counts_row)
    starts = ends - counts_row
    places = jnp.arange(length, dtype=jnp.int32)
    member = (places[:, None] >= starts[None, :]) & (places[:, None] < ends[None, :])
    labels = jnp.arange(counts_row.shape[0], dtype=jnp.int32)
    prefix_group = jnp.sum(jnp.where(member, labels[None, :], 0), axis=1)
    offset = places - jnp.sum(jnp.where(member, starts[None, :], 0), axis=1)
    return (starts, prefix_group, offset)


def attend(query_vectors, keys, values, allowed):
    scores = lax.dot_general(
        query_vectors, keys, (((1,), (1,)), ((), ())), preferred_element_type=jnp.float32
    )
    scores = scores * (1.0 / query_vectors.shape[-1] ** 0.5)
    if allowed is not None:
        scores = jnp.where(allowed, scores, -1e30)
    top = jnp.max(scores, axis=1, keepdims=True)
    expo = jnp.exp(scores - top)
    total = jnp.sum(expo, axis=1, keepdims=True)
    weights = (expo / total).astype(jnp.bfloat16)
    result = jnp.dot(weights, values, preferred_element_type=jnp.float32)
    return (result, top[:, 0] + jnp.log(total[:, 0]))


def shards(
    hidden,
    norm_gain,
    w_query,
    key_value_weight,
    w_out,
    prefix_key_cache,
    prefix_owner,
    token_counts,
):
    tensor_index = lax.axis_index("tensor")
    tensor_count = lax.axis_size("tensor")
    seq_count = lax.axis_size("seq")
    length = hidden.shape[0]
    head_size = HEAD_DIM
    whole = lax.all_gather(hidden, "tensor", axis=1, tiled=True)
    wide = whole.astype(jnp.float32)
    normalized_input = (
        wide
        * lax.rsqrt(jnp.mean(wide * wide, axis=1, keepdims=True) + eps)
        * norm_gain.astype(jnp.float32)
    ).astype(jnp.bfloat16)
    width_query = w_query.shape[1]
    full_width = key_value_weight.shape[1]
    heads_dev = width_query // head_size
    kv_heads = full_width // (2 * head_size)
    group_full = heads_dev * tensor_count // kv_heads
    kv_local = max(1, heads_dev // group_full)
    kv_start = tensor_index * heads_dev // group_full
    kv_width = kv_local * 2 * head_size
    kv_piece = lax.dynamic_slice_in_dim(key_value_weight, kv_start * 2 * head_size, kv_width, 1)
    packed = jnp.concatenate([w_query, kv_piece, w_out.T], axis=1)
    gathered = lax.all_gather(packed, "seq", axis=0, tiled=True)
    wq_full = gathered[:, :width_query]
    kv_full = gathered[:, width_query : width_query + kv_width]
    wo_cols = gathered[:, width_query + kv_width :]

    def contract(piece):
        return jnp.dot(normalized_input, piece, preferred_element_type=jnp.float32)

    query_vectors = contract(wq_full)
    key_value_pair = contract(kv_full)
    counts = token_counts[0]
    num_groups = counts.shape[0]
    starts, prefix_group, offset = layout(counts, length)
    positions = PREFIX_LENGTH + offset
    query_vectors = rotate(query_vectors.reshape(length, heads_dev, head_size), positions).astype(
        jnp.bfloat16
    )
    pair_blocks = key_value_pair.reshape(length, kv_local, 2, head_size)
    rotated_keys = rotate(pair_blocks[:, :, 0], positions)
    suffix_mine = jnp.stack([rotated_keys, pair_blocks[:, :, 1]], axis=2).astype(jnp.bfloat16)
    share = full_width // tensor_count
    suffix_flat = suffix_mine.reshape(length, kv_width)
    suffix_part = lax.dynamic_slice_in_dim(
        suffix_flat, tensor_index * share - kv_start * 2 * head_size, share, 1
    )
    suffix_keys = suffix_mine[:, :, 0]
    suffix_values = suffix_mine[:, :, 1]
    cache_all = prefix_key_cache[0].reshape(-1, kv_heads, 2, head_size)
    cache_mine = lax.dynamic_slice_in_dim(cache_all, kv_start, kv_local, 1)
    cache_keys = cache_mine[:, :, 0]
    cache_values = cache_mine[:, :, 1]
    group_width = heads_dev // kv_local
    capacity = 2 * length // seq_count
    labels = jnp.arange(num_groups, dtype=jnp.int32)
    owner_match = prefix_owner[None, :] == jnp.arange(seq_count, dtype=jnp.int32)[:, None]
    owner_start = jnp.sum(jnp.where(owner_match, starts[None, :], 0), axis=1)
    owner_count = jnp.sum(jnp.where(owner_match, counts[None, :], 0), axis=1)
    slots = jnp.arange(capacity, dtype=jnp.int32)
    valid = slots[None, :] < owner_count[:, None]
    source_rows = jnp.where(valid, owner_start[:, None] + slots[None, :], 0)
    flat_query = query_vectors.reshape(length, width_query)
    outgoing = jnp.where(valid[:, :, None], flat_query[source_rows], jnp.zeros((), jnp.bfloat16))
    arrived = lax.all_to_all(outgoing, "seq", split_axis=0, concat_axis=0, tiled=True)
    items = arrived.shape[1]
    rows_in = arrived.reshape(seq_count * items, heads_dev, head_size)
    outs = []
    logs = []
    for serve_head in range(heads_dev):
        serve_result, serve_logsum = attend(
            rows_in[:, serve_head],
            cache_keys[:, serve_head // group_width],
            cache_values[:, serve_head // group_width],
            None,
        )
        outs.append(serve_result)
        logs.append(serve_logsum)
    out_block = jnp.stack(outs, axis=1).astype(jnp.bfloat16).reshape(seq_count, items, width_query)
    log_block = jnp.stack(logs, axis=1).reshape(seq_count, items, heads_dev)
    prefix_out = lax.all_to_all(out_block, "seq", split_axis=0, concat_axis=0, tiled=True)
    prefix_log = lax.all_to_all(
        log_block.astype(jnp.bfloat16), "seq", split_axis=0, concat_axis=0, tiled=True
    ).astype(log_block.dtype)
    owner_of_token = jnp.sum(
        jnp.where(prefix_group[:, None] == labels[None, :], prefix_owner[None, :], 0), axis=1
    )
    back_rows = owner_of_token * capacity + offset
    prefix_rows = prefix_out.reshape(seq_count * capacity, heads_dev, head_size)[back_rows]
    prefix_logsum = prefix_log.reshape(seq_count * capacity, heads_dev)[back_rows]
    places = jnp.arange(length, dtype=jnp.int32)
    allowed = (prefix_group[:, None] == prefix_group[None, :]) & (
        places[None, :] <= places[:, None]
    )
    outs = []
    logs = []
    for head in range(heads_dev):
        result, logsum = attend(
            query_vectors[:, head],
            suffix_keys[:, head // group_width],
            suffix_values[:, head // group_width],
            allowed,
        )
        outs.append(result)
        logs.append(logsum)
    suffix_attn = jnp.stack(outs, axis=1)
    suffix_logsum = jnp.stack(logs, axis=1)
    upper = jnp.maximum(prefix_logsum, suffix_logsum)
    left = jnp.exp(prefix_logsum - upper)[..., None]
    right = jnp.exp(suffix_logsum - upper)[..., None]
    context = (
        (left * prefix_rows.astype(jnp.float32) + right * suffix_attn) / (left + right)
    ).astype(jnp.bfloat16)
    context = context.reshape(length, width_query)
    partial_out = lax.dot_general(
        context, wo_cols, (((1,), (1,)), ((), ())), preferred_element_type=jnp.float32
    )
    attn_out = lax.psum_scatter(
        partial_out.astype(jnp.bfloat16), "tensor", scatter_dimension=1, tiled=True
    )
    return (attn_out, suffix_part)


def solution(mesh):
    in_specs = (
        P("seq", "tensor"),
        P(),
        P("seq", "tensor"),
        P("seq", None),
        P("tensor", "seq"),
        P("seq", None, None),
        P(),
        P("seq", None),
    )
    out_specs = (P("seq", "tensor"), P("seq", "tensor"))
    return jax.shard_map(shards, mesh=mesh, in_specs=in_specs, out_specs=out_specs, check_vma=False)
```

profile of v0, /device:TPU:8, one launch (start us, length us, event | category | flops | bytes accessed | tf_op | source)
XLA Modules:
  0.0 344.0 jit_solution(9256899727202618528)
XLA Ops:
  7.2 0.7 all-gather.3.cloned.1.call-update
  8.1 1.5 pad_maximum_fusion.1
  9.6 0.7 convert_element_type.81
  10.4 0.8 copy.118
  11.3 0.7 fusion.64
  12.0 0.8 select_reduce_fusion.4
  13.0 2.9 copy.121
  16.2 0.3 copy-done.6
  16.6 1.0 multiply_cosine_fusion.1
  17.5 28.1 %all-gather.3.cloned.1.call-done = bf16[128,4096]{1,0:T(8,128)(2,1)} async-done(((bf16[128,512]{1,0:T(8,128)(2,1)}), bf16[128,4096]{1,0:T(8,128)(2,1)}) %all-gather.3.cloned.1.call-update) | async-done | bytes 1048592 | tf_op jit(solution)/shard_map/all_gather | solution.py:66
  45.6 1.5 fusion.3
  47.1 163.3 %all-gather.5.cloned.1.call-done = bf16[4096,1280]{1,0:T(8,128)(2,1)} async-done(((bf16[64,1280]{1,0:T(8,128)(2,1)}), bf16[4096,1280]{1,0:T(8,128)(2,1)}) %all-gather.5.cloned.1.call-update) | async-done | bytes 10485776 | tf_op jit(solution)/shard_map/all_gather | solution.py:83
  210.5 4.0 %fusion.1 = f32[128,512]{1,0:T(8,128)} fusion(bf16[4096,1280]{1,0:T(8,128)(2,1)} %all-gather.5.cloned.1.call-done, bf16[128,4096]{1,0:T(8,128)(2,1)} %all-gather.3.cloned.1.call-done, f32[4096]{0:T(1024)S(1)} %convert_element_type.81, f32[128]{0:T(128)S(1)} %add_rsqrt_fusion), kind=kOutput, calls=%fused_computation.5 | convolution fusion | flops 538968064 | bytes 5521920 | tf_op jit(solution)/shard_map/dot_general | solution.py:89
  214.5 1.0 reshape.627
  215.6 2.8 fusion.6
  218.3 1.0 reshape.633
  219.4 1.0 fusion.29
  220.4 0.2 fusion.70
  220.6 0.9 multiply_subtract_fusion
  221.8 0.2 fusion.72
  222.0 1.2 gather_fusion
  223.2 0.9 broadcast_select_fusion
  224.1 10.2 %all-to-all-start = ((bf16[64,4,512]{2,1,0:T(4,128)(2,1)}), bf16[64,4,512]{2,1,0:T(4,128)(2,1)S(1)}, u32[]{:S(2)}, u32[]{:S(2)}) async-start(bf16[64,4,512]{2,1,0:T(4,128)(2,1)} %broadcast_select_fusion), calls=%async_computation | async-start | bytes 524288 | tf_op jit(solution)/shard_map/all_to_all | solution.py:125
  234.3 0.2 fusion.73
  234.5 0.2 convolution_bitcast_fusion
  234.8 0.2 convolution_bitcast_fusion.1
  235.0 0.2 fusion.74
  235.2 0.2 fusion.75
  235.3 16.7 %all-to-all-done = bf16[64,4,512]{2,1,0:T(4,128)(2,1)S(1)} async-done(((bf16[64,4,512]{2,1,0:T(4,128)(2,1)}), bf16[64,4,512]{2,1,0:T(4,128)(2,1)S(1)}, u32[]{:S(2)}, u32[]{:S(2)}) %all-to-all-start) | async-done | bytes 262176 | tf_op jit(solution)/shard_map/all_to_all | solution.py:125
  252.2 0.4 fusion.69
  252.5 0.4 fusion.78
  252.9 0.3 fusion.17
  253.2 0.4 fusion.9
  253.6 0.4 fusion.77
  254.0 0.3 fusion.18
  254.3 0.4 fusion.10
  254.7 0.4 fusion.76
  255.1 0.3 fusion.19
  255.4 0.4 fusion.11
  255.8 0.4 fusion.79
  256.1 0.3 fusion.16
  256.4 0.4 fusion.8
  256.8 0.1 add.238
  256.9 0.1 add.240
  257.1 0.1 add.242
  257.2 0.1 add.236
  257.3 0.7 copy.123
  258.0 5.4 %all-to-all-start.1 = ((bf16[64,4,4]{1,2,0:T(4,128)(2,1)}), bf16[64,4,4]{1,2,0:T(4,128)(2,1)S(1)}, u32[]{:S(2)}, u32[]{:S(2)}) async-start(bf16[64,4,4]{1,2,0:T(4,128)(2,1)} %copy.123), calls=%async_computation.1 | async-start | bytes 131072 | tf_op jit(solution)/shard_map/all_to_all | solution.py:142
  263.5 0.2 copy.132
  263.7 0.8 convert_element_type.91
  264.6 13.0 %all-to-all-done.1 = bf16[64,4,4]{1,2,0:T(4,128)(2,1)S(1)} async-done(((bf16[64,4,4]{1,2,0:T(4,128)(2,1)}), bf16[64,4,4]{1,2,0:T(4,128)(2,1)S(1)}, u32[]{:S(2)}, u32[]{:S(2)}) %all-to-all-start.1) | async-done | bytes 2080 | tf_op jit(solution)/shard_map/all_to_all | solution.py:142
  277.6 5.5 %all-to-all-start.2 = ((bf16[64,4,512]{2,1,0:T(4,128)(2,1)}), bf16[64,4,512]{2,1,0:T(4,128)(2,1)S(1)}, u32[]{:S(2)}, u32[]{:S(2)}) async-start(bf16[64,4,512]{2,1,0:T(4,128)(2,1)} %convert_element_type.91), calls=%async_computation.2 | async-start | bytes 524288 | tf_op jit(solution)/shard_map/all_to_all | solution.py:141
  283.3 0.2 convolution_bitcast_fusion.2
  283.5 0.2 convolution_bitcast_fusion.3
  283.7 0.1 copy.124
  283.8 0.1 copy.136
  284.0 0.6 gather_fusion.1
  284.7 16.4 %all-to-all-done.2 = bf16[64,4,512]{2,1,0:T(4,128)(2,1)S(1)} async-done(((bf16[64,4,512]{2,1,0:T(4,128)(2,1)}), bf16[64,4,512]{2,1,0:T(4,128)(2,1)S(1)}, u32[]{:S(2)}, u32[]{:S(2)}) %all-to-all-start.2) | async-done | bytes 262176 | tf_op jit(solution)/shard_map/all_to_all | solution.py:141
  301.2 0.7 gather_fusion.2
  302.0 0.1 copy.133
  302.2 4.7 %convolution_convert_fusion = bf16[128,4096]{1,0:T(8,128)(2,1)} fusion(bf16[128,512]{0,1:T(8,128)(2,1)S(1)} %bitcast.161, bf16[4096,1280]{1,0:T(8,128)(2,1)} %all-gather.5.cloned.1.call-done), kind=kOutput, calls=%fused_computation.3 | convolution fusion | flops 537395200 | bytes 5373952 | tf_op jit(solution)/shard_map/dot_general | solution.py:175
  306.9 0.1 copy.134
  307.0 0.7 copy.135
  307.7 29.7 %reduce-scatter.2.cloned.1.call-done = bf16[128,512]{1,0:T(8,128)(2,1)} async-done(((bf16[128,4096]{1,0:T(8,128)(2,1)}), bf16[128,512]{1,0:T(8,128)(2,1)}) %reduce-scatter.2.cloned.1.call-update) | async-done | bytes 131088 | tf_op jit(solution)/shard_map/reduce_scatter | solution.py:178
  (60 shorter events, 2.0 us)
Async XLA Ops:
  7.2 0.9 copy-start
  7.2 38.4 %all-gather.3.cloned.1.call-start = ((), (), s32[]{:S(2)}) async-start(), calls=%async_computation.4 | async-start | bytes 1179648 | tf_op jit(solution)/shard_map/all_gather | solution.py:66
  7.9 202.5 %all-gather.5.cloned.1.call-start = ((), (), s32[]{:S(2)}) async-start(), calls=%async_computation.5 | async-start | bytes 10649600 | tf_op jit(solution)/shard_map/all_gather | solution.py:83
  10.3 200.1 %copy-start.2 = (f32[4096]{0:T(1024)}, f32[4096]{0:T(1024)S(1)}, u32[]{:S(2)}) copy-start(f32[4096]{0:T(1024)S(1)} %convert_element_type.81) | copy-start | bytes 49156
  13.0 3.0 copy-start.5
  15.9 194.6 %copy-start.3 = (f32[64]{0:T(128)}, f32[64]{0:T(128)S(1)}, u32[]{:S(2)}) copy-start(f32[64]{0:T(128)S(1)} %multiply_power_fusion) | copy-start | bytes 772
  16.0 0.6 copy-start.6
  16.1 194.3 %copy-start.4 = (f32[128]{0:T(128)}, f32[128]{0:T(128)S(1)}, u32[]{:S(2)}) copy-start(f32[128]{0:T(128)S(1)} %add_convert_fusion.4) | copy-start | bytes 1540
  47.1 163.4 %copy-start.8 = (f32[128]{0:T(128)}, f32[128]{0:T(128)S(1)}, u32[]{:S(2)}) copy-start(f32[128]{0:T(128)S(1)} %add_rsqrt_fusion) | copy-start | bytes 1540
  47.1 168.4 %copy-start.1 = (bf16[128,4096]{1,0:T(8,128)(2,1)S(1)}, bf16[128,4096]{1,0:T(8,128)(2,1)}, u32[]{:S(2)}) copy-start(bf16[128,4096]{1,0:T(8,128)(2,1)} %all-gather.3.cloned.1.call-done) | copy-start | bytes 3145732
  218.3 3.5 %copy-start.7 = (s32[128]{0:T(128)S(1)}, s32[128]{0:T(128)}, u32[]{:S(2)}) copy-start(s32[128]{0:T(128)} %copy-done.6) | copy-start | bytes 1540
  224.1 27.9 %all-to-all-start = ((bf16[64,4,512]{2,1,0:T(4,128)(2,1)}), bf16[64,4,512]{2,1,0:T(4,128)(2,1)S(1)}, u32[]{:S(2)}, u32[]{:S(2)}) async-start(bf16[64,4,512]{2,1,0:T(4,128)(2,1)} %broadcast_select_fusion), calls=%async_computation | async-start | bytes 524288 | tf_op jit(solution)/shard_map/all_to_all | solution.py:125
  258.0 19.6 %all-to-all-start.1 = ((bf16[64,4,4]{1,2,0:T(4,128)(2,1)}), bf16[64,4,4]{1,2,0:T(4,128)(2,1)S(1)}, u32[]{:S(2)}, u32[]{:S(2)}) async-start(bf16[64,4,4]{1,2,0:T(4,128)(2,1)} %copy.123), calls=%async_computation.1 | async-start | bytes 131072 | tf_op jit(solution)/shard_map/all_to_all | solution.py:142
  277.6 23.5 %all-to-all-start.2 = ((bf16[64,4,512]{2,1,0:T(4,128)(2,1)}), bf16[64,4,512]{2,1,0:T(4,128)(2,1)S(1)}, u32[]{:S(2)}, u32[]{:S(2)}) async-start(bf16[64,4,512]{2,1,0:T(4,128)(2,1)} %convert_element_type.91), calls=%async_computation.2 | async-start | bytes 524288 | tf_op jit(solution)/shard_map/all_to_all | solution.py:141
  283.1 54.3 %reduce-scatter.2.cloned.1.call-start = ((), (), s32[]{:S(2)}) async-start(), calls=%async_computation.6 | async-start | bytes 1179648 | tf_op jit(solution)/shard_map/reduce_scatter | solution.py:178
Sparse Core Ops, SparseCore 0:
  10.1 35.3 all-gather.2
  48.5 161.8 all-gather.4
  307.0 30.4 reduce-scatter.1
where the time goes:
time: 345 us; the launch traced here: 344 us
  waiting for transfers between devices  268 us (78%)
  starting transfers between devices  21.3 us (6%)
  matrix products  16 us (5%)
  between operations  14.2 us (4%)
  local copies, waits for them, and re-layouts  13.2 us (4%)
  other arithmetic  11.4 us (3%)
    all_gather x1, waiting for transfers between devices, shards(): gathered = lax.all_gather(packed, 'seq', axis=0, tiled=True)  163 us
    reduce_scatter x1, waiting for transfers between devices, shards(): lax.psum_scatter(partial_out.astype(jnp.bfloat16), 'tensor', scatter_dime...  29.7 us
    all_gather x1, waiting for transfers between devices, shards(): whole = lax.all_gather(hidden, 'tensor', axis=1, tiled=True)  28.1 us
    all_to_all x1, waiting for transfers between devices, shards(): lax.all_to_all(outgoing, 'seq', split_axis=0, concat_axis=0, tiled=True)  16.7 us
    all_to_all x1, waiting for transfers between devices, shards(): lax.all_to_all(out_block, 'seq', split_axis=0, concat_axis=0, tiled=True)  16.4 us
    all_to_all x1, waiting for transfers between devices, shards(): lax.all_to_all(log_block.astype(jnp.bfloat16), 'seq', split_axis=0, conca...  13 us
    all_to_all x1, starting transfers between devices, shards(): lax.all_to_all(outgoing, 'seq', split_axis=0, concat_axis=0, tiled=True)  10.2 us
  transfers between devices with their start and end apart: 6, of which 6 were waited for; matrix products, arithmetic and copies ran while one was open for 4% of the time, Pallas kernels for 0%

commit v1 on v0

--- a/solution.py
+++ b/solution.py
@@ -63,7 +63,13 @@
     seq_count = lax.axis_size("seq")
     length = hidden.shape[0]
     head_size = HEAD_DIM
-    whole = lax.all_gather(hidden, "tensor", axis=1, tiled=True)
+    size = lax.axis_size("tensor")
+    held, blocks = (hidden, [hidden])
+    for _ in range(size - 1):
+        held = lax.ppermute(held, "tensor", [(i, (i + 1) % size) for i in range(size)])
+        blocks.insert(0, held)
+    line = jnp.concatenate(blocks, axis=1)
+    whole = jnp.roll(line, (lax.axis_index("tensor") + 1) * hidden.shape[1], axis=1)
     wide = whole.astype(jnp.float32)
     normalized_input = (
         wide

time: 345 us -> 307 us (0.89)
  waiting for transfers between devices: 268 us -> 234 us
    all_gather x1, waiting for transfers between devices: 163 us -> 126 us  [shards(): gathered = lax.all_gather(packed, 'seq', axis=0, tiled=True)]
    ppermute x0 -> x7, waiting for transfers between devices: none -> 31.9 us  [shards(): lax.ppermute(held, 'tensor', [(i, (i + 1) % size) for i in range(size)])]
    all_gather x1 -> x0, waiting for transfers between devices: 28.1 us -> none  [shards(): whole = lax.all_gather(hidden, 'tensor', axis=1, tiled=True)]
  transfers between devices with their start and end apart: 6 -> 12, of which waited for: 6 -> 12; matrix products, arithmetic and copies ran while one was open for 4% -> 4% of each run, Pallas kernels for 0% -> 0%
where the time goes in v1:
time: 307 us
  waiting for transfers between devices  234 us (76%)
  starting transfers between devices  21.4 us (7%)
  matrix products  14.9 us (5%)
  between operations  14.6 us (5%)
  local copies, waits for them, and re-layouts  13.2 us (4%)
  other arithmetic  8.66 us (3%)
    all_gather x1, waiting for transfers between devices, shards(): gathered = lax.all_gather(packed, 'seq', axis=0, tiled=True)  126 us
    ppermute x7, waiting for transfers between devices, shards(): lax.ppermute(held, 'tensor', [(i, (i + 1) % size) for i in range(size)])  31.9 us
    reduce_scatter x1, waiting for transfers between devices, shards(): lax.psum_scatter(partial_out.astype(jnp.bfloat16), 'tensor', scatter_dime...  29.7 us
    all_to_all x1, waiting for transfers between devices, shards(): lax.all_to_all(outgoing, 'seq', split_axis=0, concat_axis=0, tiled=True)  16.7 us
    all_to_all x1, waiting for transfers between devices, shards(): lax.all_to_all(out_block, 'seq', split_axis=0, concat_axis=0, tiled=True)  16.4 us
    all_to_all x1, waiting for transfers between devices, shards(): lax.all_to_all(log_block.astype(jnp.bfloat16), 'seq', split_axis=0, conca...  13 us
    all_to_all x1, starting transfers between devices, shards(): lax.all_to_all(outgoing, 'seq', split_axis=0, concat_axis=0, tiled=True)  10.1 us
  transfers between devices with their start and end apart: 12, of which 12 were waited for; matrix products, arithmetic and copies ran while one was open for 4% of the time, Pallas kernels for 0%

profile of v1, /device:TPU:8, one launch (start us, length us, event | category | flops | bytes accessed | tf_op | source)
XLA Modules:
  0.0 306.7 jit_solution(10967625061668797095)
XLA Ops:
  7.2 0.8 copy-done
  8.1 1.6 pad_maximum_fusion.1
  9.7 0.7 copy.118
  10.6 0.7 fusion.66
  11.4 4.1 %collective-permute-done = bf16[128,512]{1,0:T(8,128)(2,1)S(1)} collective-permute-done((bf16[128,512]{1,0:T(8,128)(2,1)}, bf16[128,512]{1,0:T(8,128)(2,1)S(1)}, u32[]{:S(2)}, u32[]{:S(2)}) %collective-permute-start) | collective-permute-done | bytes 131104 | tf_op jit(solution)/shard_map/ppermute | solution.py:69
  15.5 5.6 %collective-permute-done.1 = bf16[128,512]{1,0:T(8,128)(2,1)S(1)} collective-permute-done((bf16[128,512]{1,0:T(8,128)(2,1)S(1)}, bf16[128,512]{1,0:T(8,128)(2,1)S(1)}, u32[]{:S(2)}, u32[]{:S(2)}) %collective-permute-start.1) | collective-permute-done | bytes 131104 | tf_op jit(solution)/shard_map/ppermute | solution.py:69
  21.1 0.3 multiply_cosine_fusion.1
  21.4 0.8 select_reduce_fusion.4
  22.2 4.5 %collective-permute-done.2 = bf16[128,512]{1,0:T(8,128)(2,1)S(1)} collective-permute-done((bf16[128,512]{1,0:T(8,128)(2,1)S(1)}, bf16[128,512]{1,0:T(8,128)(2,1)S(1)}, u32[]{:S(2)}, u32[]{:S(2)}) %collective-permute-start.2) | collective-permute-done | bytes 131104 | tf_op jit(solution)/shard_map/ppermute | solution.py:69
  26.8 5.5 %collective-permute-done.3 = bf16[128,512]{1,0:T(8,128)(2,1)S(1)} collective-permute-done((bf16[128,512]{1,0:T(8,128)(2,1)S(1)}, bf16[128,512]{1,0:T(8,128)(2,1)S(1)}, u32[]{:S(2)}, u32[]{:S(2)}) %collective-permute-start.3) | collective-permute-done | bytes 131104 | tf_op jit(solution)/shard_map/ppermute | solution.py:69
  32.5 0.8 select_reduce_fusion
  33.2 4.7 %collective-permute-done.4 = bf16[128,512]{1,0:T(8,128)(2,1)S(1)} collective-permute-done((bf16[128,512]{1,0:T(8,128)(2,1)S(1)}, bf16[128,512]{1,0:T(8,128)(2,1)S(1)}, u32[]{:S(2)}, u32[]{:S(2)}) %collective-permute-start.4) | collective-permute-done | bytes 131104 | tf_op jit(solution)/shard_map/ppermute | solution.py:69
  37.9 5.6 %collective-permute-done.5 = bf16[128,512]{1,0:T(8,128)(2,1)S(1)} collective-permute-done((bf16[128,512]{1,0:T(8,128)(2,1)S(1)}, bf16[128,512]{1,0:T(8,128)(2,1)S(1)}, u32[]{:S(2)}, u32[]{:S(2)}) %collective-permute-start.5) | collective-permute-done | bytes 131104 | tf_op jit(solution)/shard_map/ppermute | solution.py:69
  43.5 0.7 convert_element_type.81
  44.2 2.9 copy.121
  47.2 1.9 collective-permute-done.6
  49.4 1.3 copy-done.1
  50.7 0.3 fusion.3
  51.0 126.1 %all-gather.2.cloned.1.call-done = bf16[4096,1280]{1,0:T(8,128)(2,1)} async-done(((bf16[64,1280]{1,0:T(8,128)(2,1)}), bf16[4096,1280]{1,0:T(8,128)(2,1)}) %all-gather.2.cloned.1.call-update) | async-done | bytes 10485776 | tf_op jit(solution)/shard_map/all_gather | solution.py:89
  177.1 2.4 fusion.6
  179.7 0.3 fusion.29
  180.0 3.3 %fusion.1 = f32[128,512]{1,0:T(8,128)S(1)} fusion(bf16[4096,1280]{1,0:T(8,128)(2,1)} %all-gather.2.cloned.1.call-done, f32[4096]{0:T(1024)S(1)} %convert_element_type.81, f32[128]{0:T(128)S(1)} %add_rsqrt_fusion, bf16[128,8192]{1,0:T(8,128)(2,1)} %copy-done.1, s32[]{:T(128)S(6)} %select_n.94), kind=kOutput, calls=%fused_computation.5 | convolution fusion | flops 538968064 | bytes 5521924 | tf_op jit(solution)/shard_map/dot_general | solution.py:95
  183.4 0.2 fusion.72
  184.0 0.2 fusion.74
  184.2 1.2 gather_fusion
  185.4 0.9 broadcast_select_fusion
  186.3 10.1 %all-to-all-start = ((bf16[64,4,512]{2,1,0:T(4,128)(2,1)}), bf16[64,4,512]{2,1,0:T(4,128)(2,1)S(1)}, u32[]{:S(2)}, u32[]{:S(2)}) async-start(bf16[64,4,512]{2,1,0:T(4,128)(2,1)} %broadcast_select_fusion), calls=%async_computation | async-start | bytes 524288 | tf_op jit(solution)/shard_map/all_to_all | solution.py:131
  196.5 0.2 fusion.75
  196.7 0.2 convolution_bitcast_fusion
  196.9 0.2 convolution_bitcast_fusion.1
  197.2 0.2 fusion.76
  197.3 0.2 fusion.77
  197.5 16.7 %all-to-all-done = bf16[64,4,512]{2,1,0:T(4,128)(2,1)S(1)} async-done(((bf16[64,4,512]{2,1,0:T(4,128)(2,1)}), bf16[64,4,512]{2,1,0:T(4,128)(2,1)S(1)}, u32[]{:S(2)}, u32[]{:S(2)}) %all-to-all-start) | async-done | bytes 262176 | tf_op jit(solution)/shard_map/all_to_all | solution.py:131
  214.3 0.4 fusion.71
  214.7 0.4 fusion.78
  215.1 0.3 fusion.19
  215.4 0.4 fusion.11
  215.8 0.4 fusion.79
  216.2 0.3 fusion.18
  216.5 0.4 fusion.10
  216.9 0.4 fusion.80
  217.2 0.3 fusion.17
  217.6 0.4 fusion.9
  217.9 0.4 fusion.81
  218.3 0.3 fusion.16
  218.6 0.4 fusion.8
  219.6 0.7 copy.123
  220.2 5.4 %all-to-all-start.1 = ((bf16[64,4,4]{1,2,0:T(4,128)(2,1)}), bf16[64,4,4]{1,2,0:T(4,128)(2,1)S(1)}, u32[]{:S(2)}, u32[]{:S(2)}) async-start(bf16[64,4,4]{1,2,0:T(4,128)(2,1)} %copy.123), calls=%async_computation.1 | async-start | bytes 131072 | tf_op jit(solution)/shard_map/all_to_all | solution.py:148
  225.7 0.2 copy.132
  226.0 0.8 convert_element_type.91
  226.8 13.0 %all-to-all-done.1 = bf16[64,4,4]{1,2,0:T(4,128)(2,1)S(1)} async-done(((bf16[64,4,4]{1,2,0:T(4,128)(2,1)}), bf16[64,4,4]{1,2,0:T(4,128)(2,1)S(1)}, u32[]{:S(2)}, u32[]{:S(2)}) %all-to-all-start.1) | async-done | bytes 2080 | tf_op jit(solution)/shard_map/all_to_all | solution.py:148
  239.8 5.7 %all-to-all-start.2 = ((bf16[64,4,512]{2,1,0:T(4,128)(2,1)}), bf16[64,4,512]{2,1,0:T(4,128)(2,1)S(1)}, u32[]{:S(2)}, u32[]{:S(2)}) async-start(bf16[64,4,512]{2,1,0:T(4,128)(2,1)} %convert_element_type.91), calls=%async_computation.2 | async-start | bytes 524288 | tf_op jit(solution)/shard_map/all_to_all | solution.py:147
  245.7 0.2 convolution_bitcast_fusion.2
  245.9 0.2 convolution_bitcast_fusion.3
  246.1 0.1 copy.124
  246.2 0.1 copy.136
  246.4 0.6 gather_fusion.1
  247.1 16.4 %all-to-all-done.2 = bf16[64,4,512]{2,1,0:T(4,128)(2,1)S(1)} async-done(((bf16[64,4,512]{2,1,0:T(4,128)(2,1)}), bf16[64,4,512]{2,1,0:T(4,128)(2,1)S(1)}, u32[]{:S(2)}, u32[]{:S(2)}) %all-to-all-start.2) | async-done | bytes 262176 | tf_op jit(solution)/shard_map/all_to_all | solution.py:147
  263.6 0.7 gather_fusion.2
  264.4 0.1 copy.133
  264.6 4.7 %convolution_convert_fusion = bf16[128,4096]{1,0:T(8,128)(2,1)} fusion(bf16[128,512]{0,1:T(8,128)(2,1)S(1)} %bitcast.161, bf16[4096,1280]{1,0:T(8,128)(2,1)} %all-gather.2.cloned.1.call-done), kind=kOutput, calls=%fused_computation.3 | convolution fusion | flops 537395200 | bytes 5373952 | tf_op jit(solution)/shard_map/dot_general | solution.py:181
  269.3 0.1 copy.134
  269.4 0.7 copy.135
  270.1 29.7 %reduce-scatter.2.cloned.1.call-done = bf16[128,512]{1,0:T(8,128)(2,1)} async-done(((bf16[128,4096]{1,0:T(8,128)(2,1)}), bf16[128,512]{1,0:T(8,128)(2,1)}) %reduce-scatter.2.cloned.1.call-update) | async-done | bytes 131088 | tf_op jit(solution)/shard_map/reduce_scatter | solution.py:184
  (75 shorter events, 2.7 us)
Async XLA Ops:
  7.2 0.9 copy-start
  7.2 170.0 %all-gather.2.cloned.1.call-start = ((), (), s32[]{:S(2)}) async-start(), calls=%async_computation.4 | async-start | bytes 10649600 | tf_op jit(solution)/shard_map/all_gather | solution.py:89
  9.7 5.8 %collective-permute-start = (bf16[128,512]{1,0:T(8,128)(2,1)}, bf16[128,512]{1,0:T(8,128)(2,1)S(1)}, u32[]{:S(2)}, u32[]{:S(2)}) collective-permute-start(bf16[128,512]{1,0:T(8,128)(2,1)} %param.8), channel_id=1, source_target_pairs={{0,1},{1,2},{2,3},{3,4},{4,5},{5,6},{6,7},{7,0},{8,9},{9,10},{10,1... | collective-permute-start | bytes 393224 | tf_op jit(solution)/shard_map/ppermute | solution.py:69
  15.5 5.6 %collective-permute-start.1 = (bf16[128,512]{1,0:T(8,128)(2,1)S(1)}, bf16[128,512]{1,0:T(8,128)(2,1)S(1)}, u32[]{:S(2)}, u32[]{:S(2)}) collective-permute-start(bf16[128,512]{1,0:T(8,128)(2,1)S(1)} %collective-permute-done), channel_id=1, source_target_pairs={{0,1},{1,2},{2,3},{3,4},{4,5},{5,6},{6,7},{7,0},{8,9},{9,10},{10,1... | collective-permute-start | bytes 393224 | tf_op jit(solution)/shard_map/ppermute | solution.py:69
  21.1 5.6 %collective-permute-start.2 = (bf16[128,512]{1,0:T(8,128)(2,1)S(1)}, bf16[128,512]{1,0:T(8,128)(2,1)S(1)}, u32[]{:S(2)}, u32[]{:S(2)}) collective-permute-start(bf16[128,512]{1,0:T(8,128)(2,1)S(1)} %collective-permute-done.1), channel_id=1, source_target_pairs={{0,1},{1,2},{2,3},{3,4},{4,5},{5,6},{6,7},{7,0},{8,9},{9,10},{10,1... | collective-permute-start | bytes 393224 | tf_op jit(solution)/shard_map/ppermute | solution.py:69
  26.7 5.6 %collective-permute-start.3 = (bf16[128,512]{1,0:T(8,128)(2,1)S(1)}, bf16[128,512]{1,0:T(8,128)(2,1)S(1)}, u32[]{:S(2)}, u32[]{:S(2)}) collective-permute-start(bf16[128,512]{1,0:T(8,128)(2,1)S(1)} %collective-permute-done.2), channel_id=1, source_target_pairs={{0,1},{1,2},{2,3},{3,4},{4,5},{5,6},{6,7},{7,0},{8,9},{9,10},{10,1... | collective-permute-start | bytes 393224 | tf_op jit(solution)/shard_map/ppermute | solution.py:69
  32.3 5.6 %collective-permute-start.4 = (bf16[128,512]{1,0:T(8,128)(2,1)S(1)}, bf16[128,512]{1,0:T(8,128)(2,1)S(1)}, u32[]{:S(2)}, u32[]{:S(2)}) collective-permute-start(bf16[128,512]{1,0:T(8,128)(2,1)S(1)} %collective-permute-done.3), channel_id=1, source_target_pairs={{0,1},{1,2},{2,3},{3,4},{4,5},{5,6},{6,7},{7,0},{8,9},{9,10},{10,1... | collective-permute-start | bytes 393224 | tf_op jit(solution)/shard_map/ppermute | solution.py:69
  37.9 5.6 %collective-permute-start.5 = (bf16[128,512]{1,0:T(8,128)(2,1)S(1)}, bf16[128,512]{1,0:T(8,128)(2,1)S(1)}, u32[]{:S(2)}, u32[]{:S(2)}) collective-permute-start(bf16[128,512]{1,0:T(8,128)(2,1)S(1)} %collective-permute-done.4), channel_id=1, source_target_pairs={{0,1},{1,2},{2,3},{3,4},{4,5},{5,6},{6,7},{7,0},{8,9},{9,10},{10,1... | collective-permute-start | bytes 393224 | tf_op jit(solution)/shard_map/ppermute | solution.py:69
  43.5 5.6 %collective-permute-start.6 = (bf16[128,512]{1,0:T(8,128)(2,1)S(1)}, bf16[128,512]{1,0:T(8,128)(2,1)S(1)}, u32[]{:S(2)}, u32[]{:S(2)}) collective-permute-start(bf16[128,512]{1,0:T(8,128)(2,1)S(1)} %collective-permute-done.5), channel_id=1, source_target_pairs={{0,1},{1,2},{2,3},{3,4},{4,5},{5,6},{6,7},{7,0},{8,9},{9,10},{10,1... | collective-permute-start | bytes 393224 | tf_op jit(solution)/shard_map/ppermute | solution.py:69
  44.2 5.0 %copy-start.2 = (bf16[128,512]{1,0:T(8,128)(2,1)S(1)}, bf16[128,512]{1,0:T(8,128)(2,1)}, u32[]{:S(2)}) copy-start(bf16[128,512]{1,0:T(8,128)(2,1)} %param.8) | copy-start | bytes 393220
  49.4 1.3 copy-start.1
  186.3 27.9 %all-to-all-start = ((bf16[64,4,512]{2,1,0:T(4,128)(2,1)}), bf16[64,4,512]{2,1,0:T(4,128)(2,1)S(1)}, u32[]{:S(2)}, u32[]{:S(2)}) async-start(bf16[64,4,512]{2,1,0:T(4,128)(2,1)} %broadcast_select_fusion), calls=%async_computation | async-start | bytes 524288 | tf_op jit(solution)/shard_map/all_to_all | solution.py:131
  220.2 19.6 %all-to-all-start.1 = ((bf16[64,4,4]{1,2,0:T(4,128)(2,1)}), bf16[64,4,4]{1,2,0:T(4,128)(2,1)S(1)}, u32[]{:S(2)}, u32[]{:S(2)}) async-start(bf16[64,4,4]{1,2,0:T(4,128)(2,1)} %copy.123), calls=%async_computation.1 | async-start | bytes 131072 | tf_op jit(solution)/shard_map/all_to_all | solution.py:148
  239.8 23.7 %all-to-all-start.2 = ((bf16[64,4,512]{2,1,0:T(4,128)(2,1)}), bf16[64,4,512]{2,1,0:T(4,128)(2,1)S(1)}, u32[]{:S(2)}, u32[]{:S(2)}) async-start(bf16[64,4,512]{2,1,0:T(4,128)(2,1)} %convert_element_type.91), calls=%async_computation.2 | async-start | bytes 524288 | tf_op jit(solution)/shard_map/all_to_all | solution.py:147
  245.5 54.3 %reduce-scatter.2.cloned.1.call-start = ((), (), s32[]{:S(2)}) async-start(), calls=%async_computation.5 | async-start | bytes 1179648 | tf_op jit(solution)/shard_map/reduce_scatter | solution.py:184
Sparse Core Ops, SparseCore 0:
  11.0 166.1 all-gather.1
  269.4 30.4 reduce-scatter.1
